TPU v7x, 32 devices: a whole 2x2x4 slice. The times are simulated.
32 devices in a mesh: group: 4 (over z), member: 8 (over y, x, core).
Axes of the slice: x: 2, y: 2, z: 4, core: 2. Of those that a mesh axis runs over, the one named last changes fastest.
Arguments:
- query_feat: bfloat16 [4096, 4096], P(('group', 'member'))
- code_feat: bfloat16 [4096, 4096], P(('group', 'member'))
- projection: bfloat16 [4096, 1024], replicated
- hard_ids: int32 [32, 16], P(('group', 'member')), may hold values from 0 to 63, as said below
- loss_weight: float32 [4096], P(('group', 'member')), may hold values from 1 to 4
Outputs:
- query_grad: bfloat16 [4096, 4096], P(('group', 'member'))
- code_grad: bfloat16 [4096, 4096], P(('group', 'member'))
- projection_grad: float32 [4096, 1024], P(('group', 'member'))
Inputs may be any that keep to these rules, and one draw needn't show every extreme that they name: `hard_ids`: entry (owner device g * 8 + m) * 2 + slot names code rows of that device. A row names 16 different blocks, none of its own group; at most 8 of them lie in one group, and exactly 8 in some group of every row.
All inputs are finite; a program needn't handle non-finite values.
Results may differ from a plain program's by a relative error of at most 0.02.
Values may be sent and summed in bfloat16 or wider, within the bound.
No kernel may reach another device: no remote copies, remote signals or barrier semaphores. Data moves between devices by JAX's collectives and lax.ppermute only.
A program may use at most 128 MiB of HBM per device.

v0:
```python
import jax
import jax.numpy as jnp
from jax import lax
from jax.sharding import PartitionSpec as P

CB = 64
inverse_temp = 120.0
epsilon = 1e-06


def embed(features, projection):
    values = jnp.dot(features, projection, preferred_element_type=jnp.float32)
    inverse = lax.rsqrt(jnp.sum(values * values, axis=1) + epsilon)
    unit_vec = values * inverse[:, None]
    return (unit_vec, inverse, unit_vec.astype(jnp.bfloat16))


def norm_back(upstream, unit_vec, inverse):
    inner_prod = jnp.sum(unit_vec * upstream, axis=1, keepdims=True)
    return (inverse[:, None] * (upstream - unit_vec * inner_prod)).astype(jnp.bfloat16)


def shift_all(x, axis):
    size = lax.axis_size(axis)
    index = lax.axis_index(axis)
    got = [x]
    for s in range(1, size):
        got.append(lax.ppermute(x, axis, [(i, (i + s) % size) for i in range(size)]))
    order = (index - jnp.arange(size)) % size
    return jax.tree.map(lambda *xs: jnp.take(jnp.stack(xs, axis=0), order, axis=0), *got)


def exchange(parts, axis):
    size = lax.axis_size(axis)
    index = lax.axis_index(axis)
    got = [jnp.take(parts, index, axis=0)]
    for s in range(1, size):
        sent = jnp.take(parts, (index + s) % size, axis=0)
        got.append(lax.ppermute(sent, axis, [(i, (i + s) % size) for i in range(size)]))
    stacked = jnp.stack(got, axis=0)
    return jnp.take(stacked, (index - jnp.arange(size)) % size, axis=0)


def body(query_feat, code_feat, projection, hard_ids, loss_weight):
    groups = lax.axis_size("group")
    members = lax.axis_size("member")
    group_index = lax.axis_index("group")
    member_index = lax.axis_index("member")
    queries_dev = query_feat.shape[0]
    feat_width = query_feat.shape[1]
    emb_width = projection.shape[1]
    slot_count = queries_dev // CB
    per_group = members * slot_count
    group_span = members * queries_dev
    rows_dev = feat_width // (groups * members)
    feats = jnp.stack([query_feat, code_feat], axis=0).reshape(
        2, queries_dev, groups, members, rows_dev
    )
    feats = jnp.transpose(feats, (3, 0, 1, 2, 4))
    feat_cols = lax.all_to_all(feats, "member", split_axis=0, concat_axis=0, tiled=True)
    q_unit, q_inv, q_emb = embed(query_feat, projection)
    code_values = lax.all_gather(
        jnp.dot(code_feat, projection, preferred_element_type=jnp.float32),
        "member",
        axis=0,
        tiled=True,
    )
    c_inv = lax.rsqrt(jnp.sum(code_values * code_values, axis=1) + epsilon)
    c_unit = code_values * c_inv[:, None]
    group_codes = c_unit.astype(jnp.bfloat16)
    q_all = lax.all_to_all(
        jnp.broadcast_to(q_emb[None], (groups, queries_dev, emb_width)),
        "group",
        split_axis=0,
        concat_axis=0,
        tiled=True,
    )
    ids_all = shift_all(hard_ids[0], "group")
    block_ids = group_index * per_group + jnp.arange(per_group, dtype=jnp.int32)
    asked = jnp.any(ids_all[:, :, None] == block_ids[None, None, :], axis=1)
    own = jnp.arange(groups, dtype=jnp.int32) == group_index
    block_mask = asked | own[:, None]
    col_mask = jnp.broadcast_to(block_mask[:, :, None], (groups, per_group, CB)).reshape(
        groups, 1, group_span
    )
    scores = inverse_temp * jnp.einsum(
        "gqe,ke->gqk", q_all, group_codes, preferred_element_type=jnp.float32
    )
    scores = jnp.where(col_mask, scores, -jnp.inf)
    part_max = jnp.max(scores, axis=2)
    safe_max = jnp.where(part_max > -jnp.inf, part_max, 0.0)
    part_sum = jnp.sum(jnp.exp(scores - safe_max[:, :, None]), axis=2)
    weights_row = jnp.broadcast_to(loss_weight[None], (groups, queries_dev))
    stats = shift_all(jnp.stack([part_max, part_sum, weights_row], axis=0), "group")
    w_all = stats[:, 2, 0]
    row_max = jnp.max(stats[:, 0], axis=0)
    row_sum = jnp.sum(stats[:, 1] * jnp.exp(stats[:, 0] - row_max[None]), axis=0)
    log_total = row_max + jnp.log(row_sum)
    offsets = jnp.arange(queries_dev, dtype=jnp.int32)
    columns = jnp.arange(group_span, dtype=jnp.int32)
    positive = (columns[None, :] == (member_index * queries_dev + offsets)[:, None]).astype(
        jnp.float32
    )
    positive = positive[None] * own[:, None, None].astype(jnp.float32)
    factor = w_all * inverse_temp
    grad = (factor[:, :, None] * (jnp.exp(scores - log_total[:, :, None]) - positive)).astype(
        jnp.bfloat16
    )
    code_terms = None
    for g in range(groups):
        term = jnp.dot(grad[g].T, q_all[g], preferred_element_type=jnp.float32)
        term = jnp.where(g == group_index, term, term.astype(jnp.bfloat16).astype(jnp.float32))
        code_terms = term if code_terms is None else code_terms + term
    code_sum = code_terms.astype(jnp.bfloat16)
    grad_dq, code_sum = lax.optimization_barrier((grad, code_sum))
    code_delta = lax.psum(code_sum, "member").astype(jnp.float32)
    delta_parts = jnp.einsum(
        "gqk,ke->gqe", grad_dq, group_codes, preferred_element_type=jnp.float32
    )
    returned = exchange(delta_parts.astype(jnp.bfloat16), "group").astype(jnp.float32)
    own_part = jnp.take(delta_parts, group_index, axis=0)
    query_delta = own_part + jnp.sum(jnp.where(own[:, None, None], 0.0, returned), axis=0)
    dz_query = norm_back(query_delta, q_unit, q_inv)
    dz_code_all = norm_back(code_delta, c_unit, c_inv)
    dz_code = lax.dynamic_slice_in_dim(dz_code_all, member_index * queries_dev, queries_dev, 0)
    query_grad = jnp.einsum(
        "qe,de->qd", dz_query, projection, preferred_element_type=jnp.float32
    ).astype(jnp.bfloat16)
    code_grad = jnp.einsum(
        "qe,de->qd", dz_code, projection, preferred_element_type=jnp.float32
    ).astype(jnp.bfloat16)
    dzq_all = lax.all_to_all(
        jnp.broadcast_to(dz_query[None], (members, queries_dev, emb_width)),
        "member",
        split_axis=0,
        concat_axis=0,
        tiled=True,
    )
    dzc_all = dz_code_all.reshape(members, queries_dev, emb_width)
    proj_parts = jnp.einsum(
        "mqgr,mqe->gre", feat_cols[:, 0], dzq_all, preferred_element_type=jnp.float32
    ) + jnp.einsum("mqgr,mqe->gre", feat_cols[:, 1], dzc_all, preferred_element_type=jnp.float32)
    own_proj = jnp.take(proj_parts, group_index, axis=0)
    sent_proj = jnp.where(own[:, None, None], 0.0, proj_parts).astype(jnp.bfloat16)
    projection_grad = own_proj + lax.psum_scatter(
        sent_proj, "group", scatter_dimension=0, tiled=True
    ).reshape(rows_dev, emb_width).astype(jnp.float32)
    return (query_grad, code_grad, projection_grad)


def solution(mesh):
    return jax.shard_map(
        body,
        mesh=mesh,
        in_specs=(
            P(("group", "member"), None),
            P(("group", "member"), None),
            P(),
            P(("group", "member"), None),
            P(("group", "member")),
        ),
        out_specs=(
            P(("group", "member"), None),
            P(("group", "member"), None),
            P(("group", "member"), None),
        ),
        check_vma=False,
    )
```

profile of v0, /device:TPU:0, one launch (start us, length us, event | category | flops | bytes accessed | tf_op | source)
XLA Modules:
  0.0 204.6 jit_solution(2245639925189366476)
XLA Ops:
  7.2 5.8 %fusion.26 = f32[128,1024]{1,0:T(8,128)} fusion(bf16[128,4096]{1,0:T(8,128)(2,1)} %param.10, bf16[4096,1024]{1,0:T(8,128)(2,1)} %param.11), kind=kOutput, calls=%fused_computation.91 | convolution fusion | flops 1073741824 | bytes 9961472 | tf_op jit(solution)/shard_map/dot_general | solution.py:63
  13.1 3.1 %collective-permute-start = (s32[16]{0:T(128)S(1)}, s32[16]{0:T(128)S(1)}, u32[]{:S(2)}, u32[]{:S(2)}) collective-permute-start(s32[16]{0:T(128)S(1)} %bitcast.128), channel_id=1, source_target_pairs={{0,8},{8,16},{16,24},{24,0},{1,9},{9,17},{17,25},{25,1},{2,10},{10... | collective-permute-start | bytes 200 | tf_op jit(solution)/shard_map/ppermute | solution.py:28
  16.2 2.6 %collective-permute-start.1 = (s32[16]{0:T(128)S(1)}, s32[16]{0:T(128)S(1)}, u32[]{:S(2)}, u32[]{:S(2)}) collective-permute-start(s32[16]{0:T(128)S(1)} %bitcast.129), channel_id=1, source_target_pairs={{0,16},{8,24},{16,0},{24,8},{1,17},{9,25},{17,1},{25,9},{2,18},{10... | collective-permute-start | bytes 200 | tf_op jit(solution)/shard_map/ppermute | solution.py:28
  20.2 5.0 %multiply_reduce_fusion.2 = (f32[128]{0:T(128)S(1)}, f32[128,1024]{1,0:T(8,128)S(1)}) fusion(bf16[128,4096]{1,0:T(8,128)(2,1)S(1)} %copy-done.5, bf16[4096,1024]{1,0:T(8,128)(2,1)} %param.11), kind=kOutput, calls=%fused_computation.31 | convolution fusion | flops 1074003840 | bytes 9961984 | tf_op jit(solution)/shard_map/dot_general | solution.py:12
  26.4 3.6 %all-to-all-start = ((bf16[4,128,1024]{2,1,0:T(8,128)(2,1)}), bf16[4,128,1024]{2,1,0:T(8,128)(2,1)S(1)}, u32[]{:S(2)}, u32[]{:S(2)}) async-start(bf16[4,128,1024]{2,1,0:T(8,128)(2,1)} %broadcast_in_dim.126), calls=%async_computation | async-start | bytes 2097152 | tf_op jit(solution)/shard_map/all_to_all | solution.py:71
  37.5 15.0 %all-gather.2.cloned.1.call-done = f32[1024,1024]{1,0:T(8,128)} async-done(((f32[128,1024]{1,0:T(8,128)}), f32[1024,1024]{1,0:T(8,128)}) %all-gather.2.cloned.1.call-update) | async-done | bytes 4194320 | tf_op jit(solution)/shard_map/all_gather | solution.py:62
  52.6 2.5 %multiply_reduce_fusion = f32[1024]{0:T(1024)S(1)} fusion(f32[1024,1024]{1,0:T(8,128)} %all-gather.2.cloned.1.call-done), kind=kLoop, calls=%fused_computation.11 | loop fusion | flops 2096128 | bytes 4198400 | tf_op jit(solution)/shard_map/reduce_sum | solution.py:68
  55.1 4.4 %all-to-all-start.1 = ((bf16[8,2,128,4,128]{2,4,3,1,0:T(8,128)(2,1)}), bf16[8,2,128,4,128]{2,4,3,1,0:T(8,128)(2,1)}, u32[]{:S(2)}, u32[]{:S(2)}) async-start(bf16[8,2,128,4,128]{2,4,3,1,0:T(8,128)(2,1)} %copy.25), calls=%async_computation.1 | async-start | bytes 4194304 | tf_op jit(solution)/shard_map/all_to_all | solution.py:60
  59.5 3.6 %fusion.24 = (f32[4,128]{1,0:T(4,128)S(1)}, f32[4,128,1024]{2,1,0:T(8,128)S(1)}) fusion(bf16[4,128,1024]{2,1,0:T(8,128)(2,1)S(1)} %all-to-all-done, f32[1024,1024]{1,0:T(8,128)} %all-gather.2.cloned.1.call-done, f32[1024]{0:T(1024)S(1)} %add_rsqrt_fusion, pred[4,1024]{1,0:T(4,128)(4,1)S(1)} %broadcast_in_dim.124), kind=kOutput, calls=%fused_computation.89 | convolution fusion | flops 1077411328 | bytes 7350272 | tf_op jit(solution)/shard_map/gqe,ke->gqk/dot_general | solution.py:86
  69.9 3.2 %collective-permute-done.3 = f32[3,4,128]{2,1,0:T(4,128)S(1)} collective-permute-done((f32[3,4,128]{2,1,0:T(4,128)S(1)}, f32[3,4,128]{2,1,0:T(4,128)S(1)}, u32[]{:S(2)}, u32[]{:S(2)}) %collective-permute-start.3) | collective-permute-done | bytes 6176 | tf_op jit(solution)/shard_map/ppermute | solution.py:28
  80.1 3.8 %fusion.25 = (bf16[4,128,1024]{2,1,0:T(8,128)(2,1)S(1)}, f32[4,128,1024]{2,1,0:T(8,128)S(1)}) fusion(bf16[4,128,1024]{2,1,0:T(8,128)(2,1)} %copy-done.1, f32[1024,1024]{1,0:T(8,128)} %all-gather.2.cloned.1.call-done, f32[1024]{0:T(1024)S(1)} %add_rsqrt_fusion), kind=kOutput, calls=%fused_computation.90 | convolution fusion | flops 1076363264 | bytes 8392704 | tf_op jit(solution)/shard_map/gqk,ke->gqe/dot_general | solution.py:117
  85.4 3.3 %collective-permute-start.8 = (bf16[128,1024]{1,0:T(8,128)(2,1)}, bf16[128,1024]{1,0:T(8,128)(2,1)S(1)}, u32[]{:S(2)}, u32[]{:S(2)}) collective-permute-start(bf16[128,1024]{1,0:T(8,128)(2,1)} %get-tuple-element.34), channel_id=1, source_target_pairs={{0,24},{8,0},{16,8},{24,16},{1,25},{9,1},{17,9},{25,17},{2,26},{10... | collective-permute-start | bytes 786440 | tf_op jit(solution)/shard_map/ppermute | solution.py:39
  88.7 7.4 %collective-permute-done.6 = bf16[128,1024]{1,0:T(8,128)(2,1)S(1)} collective-permute-done((bf16[128,1024]{1,0:T(8,128)(2,1)}, bf16[128,1024]{1,0:T(8,128)(2,1)S(1)}, u32[]{:S(2)}, u32[]{:S(2)}) %collective-permute-start.6) | collective-permute-done | bytes 262176 | tf_op jit(solution)/shard_map/ppermute | solution.py:39
  96.2 8.9 %collective-permute-done.7 = bf16[128,1024]{1,0:T(8,128)(2,1)S(1)} collective-permute-done((bf16[128,1024]{1,0:T(8,128)(2,1)}, bf16[128,1024]{1,0:T(8,128)(2,1)S(1)}, u32[]{:S(2)}, u32[]{:S(2)}) %collective-permute-start.7) | collective-permute-done | bytes 262176 | tf_op jit(solution)/shard_map/ppermute | solution.py:39
  106.2 2.9 %gather_fusion.2 = bf16[4,128,1024]{2,1,0:T(8,128)(2,1)} fusion(bf16[4,128,1024]{2,1,0:T(8,128)(2,1)} %pad_maximum_fusion, s32[1024]{0:T(1024)S(1)} %pad_clamp_fusion), kind=kCustom, calls=%fused_computation.2 | custom fusion | bytes 2097168 | tf_op jit(solution)/shard_map/jit(_take)/gather | solution.py:41
  112.7 4.3 %all-to-all-start.2 = ((bf16[8,128,1024]{2,1,0:T(8,128)(2,1)}), bf16[8,128,1024]{2,1,0:T(8,128)(2,1)}, u32[]{:S(2)}, u32[]{:S(2)}) async-start(bf16[8,128,1024]{2,1,0:T(8,128)(2,1)} %broadcast_in_dim.134), calls=%async_computation.2 | async-start | bytes 4194304 | tf_op jit(solution)/shard_map/all_to_all | solution.py:132
  117.1 2.8 %fusion.23 = (bf16[8,1,128,4,128]{2,4,3,1,0:T(8,128)(2,1)S(1)}, bf16[8,1,128,4,128]{2,4,3,1,0:T(8,128)(2,1)}) fusion(bf16[8,2,128,4,128]{2,4,3,1,0:T(8,128)(2,1)} %all-to-all-done.1), kind=kLoop, calls=%fused_computation.88 | loop fusion | bytes 4194304 | tf_op jit(solution)/shard_map/slice | solution.py:142
  119.9 37.8 %all-reduce.2.cloned.1.call-done = bf16[1024,1024]{1,0:T(8,128)(2,1)} async-done(((bf16[1024,1024]{1,0:T(8,128)(2,1)}), bf16[1024,1024]{1,0:T(8,128)(2,1)}) %all-reduce.2.cloned.1.call-update) | async-done | bytes 2097168 | tf_op jit(solution)/shard_map/psum | solution.py:116
  157.7 3.7 %fusion = f32[1024]{0:T(1024)S(1)} fusion(bf16[1024,1024]{1,0:T(8,128)(2,1)} %all-reduce.2.cloned.1.call-done, f32[1024,1024]{1,0:T(8,128)} %all-gather.2.cloned.1.call-done, f32[1024]{0:T(1024)S(1)} %add_rsqrt_fusion), kind=kLoop, calls=%fused_computation.7 | loop fusion | flops 4193280 | bytes 6299648 | tf_op jit(solution)/shard_map/reduce_sum | solution.py:19
  163.2 3.2 %fusion.4 = f32[4,128,1024,1]{2,1,3,0:T(8,128)S(1)} fusion(bf16[8,128,1024]{2,1,0:T(8,128)(2,1)} %all-to-all-done.2, bf16[8,1,128,4,128]{2,4,3,1,0:T(8,128)(2,1)} %get-tuple-element.32), kind=kOutput, calls=%fused_computation.16 | convolution fusion | flops 1073741824 | bytes 5242880 | tf_op jit(solution)/shard_map/mqgr,mqe->gre/dot_general | solution.py:140
  166.4 2.9 %select_convert_fusion = (bf16[4,128,1024]{2,1,0:T(8,128)(2,1)}, f32[4,128,1024]{2,1,0:T(8,128)}) fusion(pred[4]{0:T(512)(128)(4,1)S(1)} %iota_compare_fusion.1, bf16[8,128,1024,1]{2,1,0,3:T(8,128)(2,1)S(1)} %bitcast.116, bf16[8,1,128,4,128]{2,4,3,1,0:T(8,128)(2,1)S(1)} %get-tuple-element.31, f32[4,128,1024,1]{2,1,3,0:T(8,128)S(1)} %fusion.4), kind=kOutput, calls=%fused_computation.18 | convolution fusion | flops 1074790400 | bytes 8388612 | tf_op jit(solution)/shard_map/mqgr,mqe->gre/dot_general | solution.py:142
  169.3 7.2 %convolution_convert_fusion.1 = bf16[128,4096]{1,0:T(8,128)(2,1)} fusion(bf16[128,1024]{1,0:T(8,128)(2,1)S(1)} %multiply_convert_fusion.2, bf16[4096,1024]{1,0:T(8,128)(2,1)} %param.11), kind=kOutput, calls=%fused_computation.6 | convolution fusion | flops 1074266112 | bytes 9699328 | tf_op jit(solution)/shard_map/qe,de->qd/dot_general | solution.py:126
  176.6 7.2 %convolution_convert_fusion = bf16[128,4096]{1,0:T(8,128)(2,1)} fusion(bf16[4096,1024]{1,0:T(8,128)(2,1)} %param.11, bf16[1024,1024]{1,0:T(8,128)(2,1)S(1)} %fusion.2, s32[]{:T(128)S(6)} %select_n.153), kind=kOutput, calls=%fused_computation.5 | convolution fusion | flops 1074266112 | bytes 9699332 | tf_op jit(solution)/shard_map/qe,de->qd/dot_general | solution.py:129
  183.8 12.3 %reduce-scatter.2.cloned.1.call-done = bf16[1,128,1024]{2,1,0:T(8,128)(2,1)} async-done(((bf16[4,128,1024]{2,1,0:T(8,128)(2,1)}), bf16[1,128,1024]{2,1,0:T(8,128)(2,1)}) %reduce-scatter.2.cloned.1.call-update) | async-done | bytes 262160 | tf_op jit(solution)/shard_map/reduce_scatter | solution.py:145
  (88 shorter events, 33.8 us)
Async XLA Ops:
  7.2 5.9 %copy-start.9 = (s32[1,16]{1,0:T(1,128)S(1)}, s32[1,16]{1,0:T(1,128)}, u32[]{:S(2)}) copy-start(s32[1,16]{1,0:T(1,128)} %param.12) | copy-start | bytes 196
  7.2 13.0 %copy-start.5 = (bf16[128,4096]{1,0:T(8,128)(2,1)S(1)}, bf16[128,4096]{1,0:T(8,128)(2,1)}, u32[]{:S(2)}) copy-start(bf16[128,4096]{1,0:T(8,128)(2,1)} %param.9) | copy-start | bytes 3145732
  7.2 45.4 %all-gather.2.cloned.1.call-start = ((), (), s32[]{:S(2)}) async-start(), calls=%async_computation.4 | async-start | bytes 4718592 | tf_op jit(solution)/shard_map/all_gather | solution.py:62
  13.1 23.4 %collective-permute-start = (s32[16]{0:T(128)S(1)}, s32[16]{0:T(128)S(1)}, u32[]{:S(2)}, u32[]{:S(2)}) collective-permute-start(s32[16]{0:T(128)S(1)} %bitcast.128), channel_id=1, source_target_pairs={{0,8},{8,16},{16,24},{24,0},{1,9},{9,17},{17,25},{25,1},{2,10},{10... | collective-permute-start | bytes 200 | tf_op jit(solution)/shard_map/ppermute | solution.py:28
  16.2 20.3 %collective-permute-start.1 = (s32[16]{0:T(128)S(1)}, s32[16]{0:T(128)S(1)}, u32[]{:S(2)}, u32[]{:S(2)}) collective-permute-start(s32[16]{0:T(128)S(1)} %bitcast.129), channel_id=1, source_target_pairs={{0,16},{8,24},{16,0},{24,8},{1,17},{9,25},{17,1},{25,9},{2,18},{10... | collective-permute-start | bytes 200 | tf_op jit(solution)/shard_map/ppermute | solution.py:28
  18.8 17.7 %collective-permute-start.2 = (s32[16]{0:T(128)S(1)}, s32[16]{0:T(128)S(1)}, u32[]{:S(2)}, u32[]{:S(2)}) collective-permute-start(s32[16]{0:T(128)S(1)} %bitcast.130), channel_id=1, source_target_pairs={{0,24},{8,0},{16,8},{24,16},{1,25},{9,1},{17,9},{25,17},{2,26},{10... | collective-permute-start | bytes 200 | tf_op jit(solution)/shard_map/ppermute | solution.py:28
  25.1 1.2 copy-start.3
  26.4 5.1 %copy-start.6 = (bf16[128,4096]{1,0:T(8,128)(2,1)S(1)}, bf16[128,4096]{1,0:T(8,128)(2,1)}, u32[]{:S(2)}) copy-start(bf16[128,4096]{1,0:T(8,128)(2,1)} %param.10) | copy-start | bytes 3145732
  26.4 28.7 %all-to-all-start = ((bf16[4,128,1024]{2,1,0:T(8,128)(2,1)}), bf16[4,128,1024]{2,1,0:T(8,128)(2,1)S(1)}, u32[]{:S(2)}, u32[]{:S(2)}) async-start(bf16[4,128,1024]{2,1,0:T(8,128)(2,1)} %broadcast_in_dim.126), calls=%async_computation | async-start | bytes 2097152 | tf_op jit(solution)/shard_map/all_to_all | solution.py:71
  31.4 1.3 copy-start.7
  55.1 56.0 %all-to-all-start.1 = ((bf16[8,2,128,4,128]{2,4,3,1,0:T(8,128)(2,1)}), bf16[8,2,128,4,128]{2,4,3,1,0:T(8,128)(2,1)}, u32[]{:S(2)}, u32[]{:S(2)}) async-start(bf16[8,2,128,4,128]{2,4,3,1,0:T(8,128)(2,1)} %copy.25), calls=%async_computation.1 | async-start | bytes 4194304 | tf_op jit(solution)/shard_map/all_to_all | solution.py:60
  59.5 98.2 %all-reduce.2.cloned.1.call-start = ((), (), s32[]{:S(2)}) async-start(), calls=%async_computation.5 | async-start | bytes 4194304 | tf_op jit(solution)/shard_map/psum | solution.py:116
  63.8 4.6 %collective-permute-start.4 = (f32[3,4,128]{2,1,0:T(4,128)S(1)}, f32[3,4,128]{2,1,0:T(4,128)S(1)}, u32[]{:S(2)}, u32[]{:S(2)}) collective-permute-start(f32[3,4,128]{2,1,0:T(4,128)S(1)} %get-tuple-element.38), channel_id=1, source_target_pairs={{0,16},{8,24},{16,0},{24,8},{1,17},{9,25},{17,1},{25,9},{2,18},{10... | collective-permute-start | bytes 18440 | tf_op jit(solution)/shard_map/ppermute | solution.py:28
  66.3 3.6 %collective-permute-start.5 = (f32[3,4,128]{2,1,0:T(4,128)S(1)}, f32[3,4,128]{2,1,0:T(4,128)S(1)}, u32[]{:S(2)}, u32[]{:S(2)}) collective-permute-start(f32[3,4,128]{2,1,0:T(4,128)S(1)} %get-tuple-element.38), channel_id=1, source_target_pairs={{0,24},{8,0},{16,8},{24,16},{1,25},{9,1},{17,9},{25,17},{2,26},{10... | collective-permute-start | bytes 18440 | tf_op jit(solution)/shard_map/ppermute | solution.py:28
  67.7 5.4 %collective-permute-start.3 = (f32[3,4,128]{2,1,0:T(4,128)S(1)}, f32[3,4,128]{2,1,0:T(4,128)S(1)}, u32[]{:S(2)}, u32[]{:S(2)}) collective-permute-start(f32[3,4,128]{2,1,0:T(4,128)S(1)} %get-tuple-element.38), channel_id=1, source_target_pairs={{0,8},{8,16},{16,24},{24,0},{1,9},{9,17},{17,25},{25,1},{2,10},{10... | collective-permute-start | bytes 18440 | tf_op jit(solution)/shard_map/ppermute | solution.py:28
  75.5 2.2 %copy-start.1 = (bf16[4,128,1024]{2,1,0:T(8,128)(2,1)}, bf16[4,128,1024]{2,1,0:T(8,128)(2,1)S(1)}, u32[]{:S(2)}) copy-start(bf16[4,128,1024]{2,1,0:T(8,128)(2,1)S(1)} %multiply_convert_fusion.1) | copy-start | bytes 3145732
  84.9 11.3 %collective-permute-start.6 = (bf16[128,1024]{1,0:T(8,128)(2,1)}, bf16[128,1024]{1,0:T(8,128)(2,1)S(1)}, u32[]{:S(2)}, u32[]{:S(2)}) collective-permute-start(bf16[128,1024]{1,0:T(8,128)(2,1)} %get-tuple-element.36), channel_id=1, source_target_pairs={{0,8},{8,16},{16,24},{24,0},{1,9},{9,17},{17,25},{25,1},{2,10},{10... | collective-permute-start | bytes 786440 | tf_op jit(solution)/shard_map/ppermute | solution.py:39
  84.9 20.2 %collective-permute-start.7 = (bf16[128,1024]{1,0:T(8,128)(2,1)}, bf16[128,1024]{1,0:T(8,128)(2,1)S(1)}, u32[]{:S(2)}, u32[]{:S(2)}) collective-permute-start(bf16[128,1024]{1,0:T(8,128)(2,1)} %get-tuple-element.35), channel_id=1, source_target_pairs={{0,16},{8,24},{16,0},{24,8},{1,17},{9,25},{17,1},{25,9},{2,18},{10... | collective-permute-start | bytes 786440 | tf_op jit(solution)/shard_map/ppermute | solution.py:39
  85.4 19.6 %collective-permute-start.8 = (bf16[128,1024]{1,0:T(8,128)(2,1)}, bf16[128,1024]{1,0:T(8,128)(2,1)S(1)}, u32[]{:S(2)}, u32[]{:S(2)}) collective-permute-start(bf16[128,1024]{1,0:T(8,128)(2,1)} %get-tuple-element.34), channel_id=1, source_target_pairs={{0,24},{8,0},{16,8},{24,16},{1,25},{9,1},{17,9},{25,17},{2,26},{10... | collective-permute-start | bytes 786440 | tf_op jit(solution)/shard_map/ppermute | solution.py:39
  106.2 4.5 %copy-start.4 = (f32[128,1024]{1,0:T(8,128)S(1)}, f32[128,1024]{1,0:T(8,128)}, u32[]{:S(2)}) copy-start(f32[128,1024]{1,0:T(8,128)} %copy-done.3) | copy-start | bytes 1572868
  112.7 50.5 %all-to-all-start.2 = ((bf16[8,128,1024]{2,1,0:T(8,128)(2,1)}), bf16[8,128,1024]{2,1,0:T(8,128)(2,1)}, u32[]{:S(2)}, u32[]{:S(2)}) async-start(bf16[8,128,1024]{2,1,0:T(8,128)(2,1)} %broadcast_in_dim.134), calls=%async_computation.2 | async-start | bytes 4194304 | tf_op jit(solution)/shard_map/all_to_all | solution.py:132
  117.1 79.1 %reduce-scatter.2.cloned.1.call-start = ((), (), s32[]{:S(2)}) async-start(), calls=%async_computation.6 | async-start | bytes 1310720 | tf_op jit(solution)/shard_map/reduce_scatter | solution.py:145
  157.7 4.0 %copy-start = (f32[1024,1024]{1,0:T(8,128)S(1)}, f32[1024,1024]{1,0:T(8,128)}, u32[]{:S(2)}) copy-start(f32[1024,1024]{1,0:T(8,128)} %all-gather.2.cloned.1.call-done) | copy-start | bytes 12582916
  157.7 4.7 %copy-start.2 = (bf16[1024,1024]{1,0:T(8,128)(2,1)S(1)}, bf16[1024,1024]{1,0:T(8,128)(2,1)}, u32[]{:S(2)}) copy-start(bf16[1024,1024]{1,0:T(8,128)(2,1)} %all-reduce.2.cloned.1.call-done) | copy-start | bytes 6291460
  (1 other events, 0.7 us)
Sparse Core Ops, SparseCore 0:
  13.2 39.2 all-gather.1
  88.8 68.7 all-reduce.1
  169.5 26.6 reduce-scatter.1
where the time goes:
time: 205 us
  waiting for transfers between devices  86.3 us (42%)
  matrix products  43.5 us (21%)
  starting transfers between devices  27.8 us (14%)
  other arithmetic  17.9 us (9%)
  local copies, waits for them, and re-layouts  15 us (7%)
  between operations  14 us (7%)
    psum x1, waiting for transfers between devices, body(): code_delta = lax.psum(code_sum, 'member').astype(jnp.float32)  37.8 us
    ppermute x3, waiting for transfers between devices, exchange(): lax.ppermute(sent, axis, [(i, (i + s) % size) for i in range(size)])  16.4 us
    all_gather x1, waiting for transfers between devices, body(): lax.all_gather(jnp.dot(code_feat, projection, preferred_element_type=jnp....  15 us
    reduce_scatter x1, waiting for transfers between devices, body(): lax.psum_scatter(sent_proj, 'group', scatter_dimension=0, tiled=True)  12.3 us
    ppermute x6, starting transfers between devices, shift_all(): lax.ppermute(x, axis, [(i, (i + s) % size) for i in range(size)])  11.5 us
    dot_general x1, matrix products, body(): jnp.einsum('qe,de->qd', dz_query, projection, preferred_element_type=jnp....  7.24 us
    dot_general x1, matrix products, body(): jnp.einsum('qe,de->qd', dz_code, projection, preferred_element_type=jnp.f...  7.24 us
    dot_general x1, matrix products, body(): jnp.dot(code_feat, projection, preferred_element_type=jnp.float32)  5.85 us
  transfers between devices with their start and end apart: 15, of which 8 were waited for; matrix products, arithmetic and copies ran while one was open for 30% of the time, Pallas kernels for 0%

commit v1 on v0

--- a/solution.py
+++ b/solution.py
@@ -113,7 +113,12 @@
         code_terms = term if code_terms is None else code_terms + term
     code_sum = code_terms.astype(jnp.bfloat16)
     grad_dq, code_sum = lax.optimization_barrier((grad, code_sum))
-    code_delta = lax.psum(code_sum, "member").astype(jnp.float32)
+
+    def begin_array(payload, group_axis):
+        view_out = jnp.sum(lax.all_gather(payload, axis_name=group_axis), 0)
+        return view_out
+
+    code_delta = begin_array(code_sum, "member").astype(jnp.float32)
     delta_parts = jnp.einsum(
         "gqk,ke->gqe", grad_dq, group_codes, preferred_element_type=jnp.float32
     )

time: 205 us -> 260 us (1.27)
  waiting for transfers between devices: 86.3 us -> 133 us
  other arithmetic: 17.9 us -> 26.7 us
    all_to_all x1, waiting for transfers between devices: 0.01 us -> 48.3 us  [body(): lax.all_to_all(jnp.broadcast_to(dz_query[None], (members, queries_dev, em...]
    psum x1 -> x0, waiting for transfers between devices: 37.8 us -> none  [body(): code_delta = lax.psum(code_sum, 'member').astype(jnp.float32)]
    all_gather x0 -> x1, waiting for transfers between devices: none -> 15.8 us  [begin_array(): view_out = jnp.sum(lax.all_gather(payload, axis_name=group_axis), 0)]
    reduce_sum x0 -> x1, other arithmetic: none -> 9.46 us  [begin_array(): view_out = jnp.sum(lax.all_gather(payload, axis_name=group_axis), 0)]
    all_to_all x1, waiting for transfers between devices: 0.01 us -> 9.05 us  [body(): lax.all_to_all(feats, 'member', split_axis=0, concat_axis=0, tiled=True)]
    all_gather x1, waiting for transfers between devices: 15 us -> 20.6 us  [body(): lax.all_gather(jnp.dot(code_feat, projection, preferred_element_type=jnp....]
    ppermute x3, waiting for transfers between devices: 16.4 us -> 21.7 us  [exchange(): lax.ppermute(sent, axis, [(i, (i + s) % size) for i in range(size)])]
  transfers between devices with their start and end apart: 15 -> 15, of which waited for: 8 -> 10; matrix products, arithmetic and copies ran while one was open for 30% -> 19% of each run, Pallas kernels for 0% -> 0%
where the time goes in v1:
time: 260 us; the launch traced here: 259 us
  waiting for transfers between devices  133 us (51%)
  matrix products  45.6 us (18%)
  other arithmetic  26.7 us (10%)
  starting transfers between devices  26 us (10%)
  local copies, waits for them, and re-layouts  14.2 us (5%)
  between operations  14.1 us (5%)
    all_to_all x1, waiting for transfers between devices, body(): lax.all_to_all(jnp.broadcast_to(dz_query[None], (members, queries_dev, em...  48.3 us
    ppermute x3, waiting for transfers between devices, exchange(): lax.ppermute(sent, axis, [(i, (i + s) % size) for i in range(size)])  21.7 us
    all_gather x1, waiting for transfers between devices, body(): lax.all_gather(jnp.dot(code_feat, projection, preferred_element_type=jnp....  20.6 us
    all_gather x1, waiting for transfers between devices, begin_array(): view_out = jnp.sum(lax.all_gather(payload, axis_name=group_axis), 0)  15.8 us
    reduce_scatter x1, waiting for transfers between devices, body(): lax.psum_scatter(sent_proj, 'group', scatter_dimension=0, tiled=True)  12.9 us
    ppermute x6, starting transfers between devices, shift_all(): lax.ppermute(x, axis, [(i, (i + s) % size) for i in range(size)])  10.6 us
    reduce_sum x1, other arithmetic, begin_array(): view_out = jnp.sum(lax.all_gather(payload, axis_name=group_axis), 0)  9.46 us
    all_to_all x1, waiting for transfers between devices, body(): lax.all_to_all(feats, 'member', split_axis=0, concat_axis=0, tiled=True)  9.05 us
  transfers between devices with their start and end apart: 15, of which 10 were waited for; matrix products, arithmetic and copies ran while one was open for 19% of the time, Pallas kernels for 0%

profile of v1, /device:TPU:0, one launch (start us, length us, event | category | flops | bytes accessed | tf_op | source)
XLA Modules:
  0.0 259.2 jit_solution(13685385001736643720)
XLA Ops:
  7.2 5.8 %fusion.26 = f32[128,1024]{1,0:T(8,128)} fusion(bf16[128,4096]{1,0:T(8,128)(2,1)} %param.10, bf16[4096,1024]{1,0:T(8,128)(2,1)} %param.11), kind=kOutput, calls=%fused_computation.91 | convolution fusion | flops 1073741824 | bytes 9961472 | tf_op jit(solution)/shard_map/dot_general | solution.py:63
  13.1 5.1 %collective-permute-start.2 = (s32[16]{0:T(128)S(1)}, s32[16]{0:T(128)S(1)}, u32[]{:S(2)}, u32[]{:S(2)}) collective-permute-start(s32[16]{0:T(128)S(1)} %bitcast.130), channel_id=1, source_target_pairs={{0,24},{8,0},{16,8},{24,16},{1,25},{9,1},{17,9},{25,17},{2,26},{10... | collective-permute-start | bytes 200 | tf_op jit(solution)/shard_map/ppermute | solution.py:28
  19.2 4.8 %multiply_reduce_fusion.2 = (f32[128]{0:T(128)S(1)}, f32[128,1024]{1,0:T(8,128)S(1)}) fusion(bf16[128,4096]{1,0:T(8,128)(2,1)S(1)} %copy-done.6, bf16[4096,1024]{1,0:T(8,128)(2,1)} %param.11), kind=kOutput, calls=%fused_computation.31 | convolution fusion | flops 1074003840 | bytes 9961984 | tf_op jit(solution)/shard_map/dot_general | solution.py:12
  26.0 4.0 %all-to-all-start = ((bf16[4,128,1024]{2,1,0:T(8,128)(2,1)}), bf16[4,128,1024]{2,1,0:T(8,128)(2,1)S(1)}, u32[]{:S(2)}, u32[]{:S(2)}) async-start(bf16[4,128,1024]{2,1,0:T(8,128)(2,1)} %broadcast_in_dim.126), calls=%async_computation | async-start | bytes 2097152 | tf_op jit(solution)/shard_map/all_to_all | solution.py:71
  32.0 20.6 %all-gather.4.cloned.1.call-done = f32[1024,1024]{1,0:T(8,128)} async-done(((f32[128,1024]{1,0:T(8,128)}), f32[1024,1024]{1,0:T(8,128)}) %all-gather.4.cloned.1.call-update) | async-done | bytes 4194320 | tf_op jit(solution)/shard_map/all_gather | solution.py:62
  52.6 2.5 multiply_reduce_fusion
  55.2 3.6 %fusion.24 = (f32[4,128]{1,0:T(4,128)S(1)}, f32[4,128,1024]{2,1,0:T(8,128)S(1)}) fusion(bf16[4,128,1024]{2,1,0:T(8,128)(2,1)S(1)} %all-to-all-done, f32[1024,1024]{1,0:T(8,128)} %all-gather.4.cloned.1.call-done, f32[1024]{0:T(1024)S(1)} %add_rsqrt_fusion, pred[4,1024]{1,0:T(4,128)(4,1)S(1)} %broadcast_in_dim.124), kind=kOutput, calls=%fused_computation.89 | convolution fusion | flops 1077411328 | bytes 7350272 | tf_op jit(solution)/shard_map/gqe,ke->gqk/dot_general | solution.py:86
  59.5 3.3 %collective-permute-start.5 = (f32[3,4,128]{2,1,0:T(4,128)S(1)}, f32[3,4,128]{2,1,0:T(4,128)S(1)}, u32[]{:S(2)}, u32[]{:S(2)}) collective-permute-start(f32[3,4,128]{2,1,0:T(4,128)S(1)} %get-tuple-element.38), channel_id=1, source_target_pairs={{0,24},{8,0},{16,8},{24,16},{1,25},{9,1},{17,9},{25,17},{2,26},{10... | collective-permute-start | bytes 18440 | tf_op jit(solution)/shard_map/ppermute | solution.py:28
  64.2 3.2 %collective-permute-done.4 = f32[3,4,128]{2,1,0:T(4,128)S(1)} collective-permute-done((f32[3,4,128]{2,1,0:T(4,128)S(1)}, f32[3,4,128]{2,1,0:T(4,128)S(1)}, u32[]{:S(2)}, u32[]{:S(2)}) %collective-permute-start.4) | collective-permute-done | bytes 6176 | tf_op jit(solution)/shard_map/ppermute | solution.py:28
  79.4 3.8 %all-to-all-start.1 = ((bf16[8,2,128,4,128]{2,4,3,1,0:T(8,128)(2,1)}), bf16[8,2,128,4,128]{2,4,3,1,0:T(8,128)(2,1)S(1)}, u32[]{:S(2)}, u32[]{:S(2)}) async-start(bf16[8,2,128,4,128]{2,4,3,1,0:T(8,128)(2,1)} %copy.25), calls=%async_computation.1 | async-start | bytes 4194304 | tf_op jit(solution)/shard_map/all_to_all | solution.py:60
  83.3 5.4 %fusion.25 = (bf16[4,128,1024]{2,1,0:T(8,128)(2,1)S(1)}, f32[4,128,1024]{2,1,0:T(8,128)}) fusion(bf16[4,128,1024]{2,1,0:T(8,128)(2,1)S(1)} %copy-done.3, f32[1024,1024]{1,0:T(8,128)} %all-gather.4.cloned.1.call-done, f32[1024]{0:T(1024)S(1)} %add_rsqrt_fusion), kind=kOutput, calls=%fused_computation.90 | convolution fusion | flops 1076363264 | bytes 8392704 | tf_op jit(solution)/shard_map/gqk,ke->gqe/dot_general | solution.py:122
  91.9 6.8 %collective-permute-done.8 = bf16[128,1024]{1,0:T(8,128)(2,1)S(1)} collective-permute-done((bf16[128,1024]{1,0:T(8,128)(2,1)S(1)}, bf16[128,1024]{1,0:T(8,128)(2,1)S(1)}, u32[]{:S(2)}, u32[]{:S(2)}) %collective-permute-start.8) | collective-permute-done | bytes 262176 | tf_op jit(solution)/shard_map/ppermute | solution.py:39
  98.7 14.9 %collective-permute-done.7 = bf16[128,1024]{1,0:T(8,128)(2,1)S(1)} collective-permute-done((bf16[128,1024]{1,0:T(8,128)(2,1)S(1)}, bf16[128,1024]{1,0:T(8,128)(2,1)S(1)}, u32[]{:S(2)}, u32[]{:S(2)}) %collective-permute-start.7) | collective-permute-done | bytes 262176 | tf_op jit(solution)/shard_map/ppermute | solution.py:39
  114.7 2.9 %gather_fusion.2 = bf16[4,128,1024]{2,1,0:T(8,128)(2,1)} fusion(bf16[4,128,1024]{2,1,0:T(8,128)(2,1)} %pad_maximum_fusion, s32[1024]{0:T(1024)S(1)} %pad_clamp_fusion), kind=kCustom, calls=%fused_computation.2 | custom fusion | bytes 2097168 | tf_op jit(solution)/shard_map/jit(_take)/gather | solution.py:41
  121.6 9.0 %all-to-all-done.1 = bf16[8,2,128,4,128]{2,4,3,1,0:T(8,128)(2,1)S(1)} async-done(((bf16[8,2,128,4,128]{2,4,3,1,0:T(8,128)(2,1)}), bf16[8,2,128,4,128]{2,4,3,1,0:T(8,128)(2,1)S(1)}, u32[]{:S(2)}, u32[]{:S(2)}) %all-to-all-start.1) | async-done | bytes 2097184 | tf_op jit(solution)/shard_map/all_to_all | solution.py:60
  132.3 4.5 %all-to-all-start.2 = ((bf16[8,128,1024]{2,1,0:T(8,128)(2,1)}), bf16[8,128,1024]{2,1,0:T(8,128)(2,1)}, u32[]{:S(2)}, u32[]{:S(2)}) async-start(bf16[8,128,1024]{2,1,0:T(8,128)(2,1)} %broadcast_in_dim.134), calls=%async_computation.2 | async-start | bytes 4194304 | tf_op jit(solution)/shard_map/all_to_all | solution.py:137
  138.0 48.3 %all-to-all-done.2 = bf16[8,128,1024]{2,1,0:T(8,128)(2,1)} async-done(((bf16[8,128,1024]{2,1,0:T(8,128)(2,1)}), bf16[8,128,1024]{2,1,0:T(8,128)(2,1)}, u32[]{:S(2)}, u32[]{:S(2)}) %all-to-all-start.2) | async-done | bytes 2097184 | tf_op jit(solution)/shard_map/all_to_all | solution.py:137
  186.3 4.5 %fusion.4 = f32[4,128,1024,1]{2,1,3,0:T(8,128)} fusion(bf16[8,128,1024]{2,1,0:T(8,128)(2,1)} %all-to-all-done.2, bf16[8,1,128,4,128]{2,4,3,1,0:T(8,128)(2,1)} %get-tuple-element.32), kind=kOutput, calls=%fused_computation.16 | convolution fusion | flops 1073741824 | bytes 5242880 | tf_op jit(solution)/shard_map/mqgr,mqe->gre/dot_general | solution.py:145
  190.8 15.8 %all-gather.6.cloned.1.call-done = bf16[8192,1024]{1,0:T(8,128)(2,1)} async-done(((bf16[1024,1024]{1,0:T(8,128)(2,1)}), bf16[8192,1024]{1,0:T(8,128)(2,1)}) %all-gather.6.cloned.1.call-update) | async-done | bytes 16777232 | tf_op jit(solution)/shard_map/all_gather | solution.py:118
  206.6 9.5 %reduce_sum.81 = bf16[1024,1024]{1,0:T(8,128)(2,1)S(1)} reduce(bf16[8,1024,1024]{2,1,0:T(8,128)(2,1)} %bitcast.117, bf16[]{:T(256)} %constant.131.clone.1), dimensions={0}, to_apply=%region_9.12 | reduce | flops 7340032 | bytes 18874370 | tf_op jit(solution)/shard_map/reduce_sum | solution.py:118
  216.1 3.0 %fusion = f32[1024]{0:T(1024)S(1)} fusion(bf16[1024,1024]{1,0:T(8,128)(2,1)S(1)} %reduce_sum.81, f32[1024,1024]{1,0:T(8,128)} %all-gather.4.cloned.1.call-done, f32[1024]{0:T(1024)S(1)} %add_rsqrt_fusion), kind=kLoop, calls=%fused_computation.7 | loop fusion | flops 4193280 | bytes 6299648 | tf_op jit(solution)/shard_map/reduce_sum | solution.py:19
  223.4 7.2 %convolution_convert_fusion.1 = bf16[128,4096]{1,0:T(8,128)(2,1)} fusion(bf16[128,1024]{1,0:T(8,128)(2,1)S(1)} %multiply_convert_fusion.2, bf16[4096,1024]{1,0:T(8,128)(2,1)} %param.11), kind=kOutput, calls=%fused_computation.6 | convolution fusion | flops 1074266112 | bytes 9699328 | tf_op jit(solution)/shard_map/qe,de->qd/dot_general | solution.py:131
  230.7 7.3 %convolution_convert_fusion = bf16[128,4096]{1,0:T(8,128)(2,1)} fusion(bf16[4096,1024]{1,0:T(8,128)(2,1)} %param.11, bf16[1024,1024]{1,0:T(8,128)(2,1)} %copy-done.1, s32[]{:T(128)S(6)} %select_n.153), kind=kOutput, calls=%fused_computation.5 | convolution fusion | flops 1074266112 | bytes 9699332 | tf_op jit(solution)/shard_map/qe,de->qd/dot_general | solution.py:134
  238.0 12.9 %reduce-scatter.2.cloned.1.call-done = bf16[1,128,1024]{2,1,0:T(8,128)(2,1)} async-done(((bf16[4,128,1024]{2,1,0:T(8,128)(2,1)}), bf16[1,128,1024]{2,1,0:T(8,128)(2,1)}) %reduce-scatter.2.cloned.1.call-update) | async-done | bytes 262160 | tf_op jit(solution)/shard_map/reduce_scatter | solution.py:150
  (93 shorter events, 36.3 us)
Async XLA Ops:
  7.2 5.9 %copy-start.11 = (s32[1,16]{1,0:T(1,128)S(1)}, s32[1,16]{1,0:T(1,128)}, u32[]{:S(2)}) copy-start(s32[1,16]{1,0:T(1,128)} %param.12) | copy-start | bytes 196
  7.2 12.1 %copy-start.6 = (bf16[128,4096]{1,0:T(8,128)(2,1)S(1)}, bf16[128,4096]{1,0:T(8,128)(2,1)}, u32[]{:S(2)}) copy-start(bf16[128,4096]{1,0:T(8,128)(2,1)} %param.9) | copy-start | bytes 3145732
  7.2 45.4 %all-gather.4.cloned.1.call-start = ((), (), s32[]{:S(2)}) async-start(), calls=%async_computation.4 | async-start | bytes 4718592 | tf_op jit(solution)/shard_map/all_gather | solution.py:62
  13.1 17.9 %collective-permute-start.2 = (s32[16]{0:T(128)S(1)}, s32[16]{0:T(128)S(1)}, u32[]{:S(2)}, u32[]{:S(2)}) collective-permute-start(s32[16]{0:T(128)S(1)} %bitcast.130), channel_id=1, source_target_pairs={{0,24},{8,0},{16,8},{24,16},{1,25},{9,1},{17,9},{25,17},{2,26},{10... | collective-permute-start | bytes 200 | tf_op jit(solution)/shard_map/ppermute | solution.py:28
  18.2 12.8 %collective-permute-start.1 = (s32[16]{0:T(128)S(1)}, s32[16]{0:T(128)S(1)}, u32[]{:S(2)}, u32[]{:S(2)}) collective-permute-start(s32[16]{0:T(128)S(1)} %bitcast.131), channel_id=1, source_target_pairs={{0,16},{8,24},{16,0},{24,8},{1,17},{9,25},{17,1},{25,9},{2,18},{10... | collective-permute-start | bytes 200 | tf_op jit(solution)/shard_map/ppermute | solution.py:28
  18.2 12.8 %collective-permute-start = (s32[16]{0:T(128)S(1)}, s32[16]{0:T(128)S(1)}, u32[]{:S(2)}, u32[]{:S(2)}) collective-permute-start(s32[16]{0:T(128)S(1)} %bitcast.132), channel_id=1, source_target_pairs={{0,8},{8,16},{16,24},{24,0},{1,9},{9,17},{17,25},{25,1},{2,10},{10... | collective-permute-start | bytes 200 | tf_op jit(solution)/shard_map/ppermute | solution.py:28
  26.0 29.2 %all-to-all-start = ((bf16[4,128,1024]{2,1,0:T(8,128)(2,1)}), bf16[4,128,1024]{2,1,0:T(8,128)(2,1)S(1)}, u32[]{:S(2)}, u32[]{:S(2)}) async-start(bf16[4,128,1024]{2,1,0:T(8,128)(2,1)} %broadcast_in_dim.126), calls=%async_computation | async-start | bytes 2097152 | tf_op jit(solution)/shard_map/all_to_all | solution.py:71
  30.0 176.6 %all-gather.6.cloned.1.call-start = ((), (), s32[]{:S(2)}) async-start(), calls=%async_computation.6 | async-start | bytes 18874368 | tf_op jit(solution)/shard_map/all_gather | solution.py:118
  59.5 4.7 %collective-permute-start.5 = (f32[3,4,128]{2,1,0:T(4,128)S(1)}, f32[3,4,128]{2,1,0:T(4,128)S(1)}, u32[]{:S(2)}, u32[]{:S(2)}) collective-permute-start(f32[3,4,128]{2,1,0:T(4,128)S(1)} %get-tuple-element.38), channel_id=1, source_target_pairs={{0,24},{8,0},{16,8},{24,16},{1,25},{9,1},{17,9},{25,17},{2,26},{10... | collective-permute-start | bytes 18440 | tf_op jit(solution)/shard_map/ppermute | solution.py:28
  62.9 4.5 %collective-permute-start.4 = (f32[3,4,128]{2,1,0:T(4,128)S(1)}, f32[3,4,128]{2,1,0:T(4,128)S(1)}, u32[]{:S(2)}, u32[]{:S(2)}) collective-permute-start(f32[3,4,128]{2,1,0:T(4,128)S(1)} %get-tuple-element.38), channel_id=1, source_target_pairs={{0,16},{8,24},{16,0},{24,8},{1,17},{9,25},{17,1},{25,9},{2,18},{10... | collective-permute-start | bytes 18440 | tf_op jit(solution)/shard_map/ppermute | solution.py:28
  62.9 5.4 %collective-permute-start.3 = (f32[3,4,128]{2,1,0:T(4,128)S(1)}, f32[3,4,128]{2,1,0:T(4,128)S(1)}, u32[]{:S(2)}, u32[]{:S(2)}) collective-permute-start(f32[3,4,128]{2,1,0:T(4,128)S(1)} %get-tuple-element.38), channel_id=1, source_target_pairs={{0,8},{8,16},{16,24},{24,0},{1,9},{9,17},{17,25},{25,1},{2,10},{10... | collective-permute-start | bytes 18440 | tf_op jit(solution)/shard_map/ppermute | solution.py:28
  70.6 2.2 copy-start.2
  75.2 1.9 copy-start.7
  79.4 3.9 %copy-start.3 = (bf16[4,128,1024]{2,1,0:T(8,128)(2,1)S(1)}, bf16[4,128,1024]{2,1,0:T(8,128)(2,1)}, u32[]{:S(2)}) copy-start(bf16[4,128,1024]{2,1,0:T(8,128)(2,1)} %copy-done.2) | copy-start | bytes 3145732
  79.4 51.3 %all-to-all-start.1 = ((bf16[8,2,128,4,128]{2,4,3,1,0:T(8,128)(2,1)}), bf16[8,2,128,4,128]{2,4,3,1,0:T(8,128)(2,1)S(1)}, u32[]{:S(2)}, u32[]{:S(2)}) async-start(bf16[8,2,128,4,128]{2,4,3,1,0:T(8,128)(2,1)} %copy.25), calls=%async_computation.1 | async-start | bytes 4194304 | tf_op jit(solution)/shard_map/all_to_all | solution.py:60
  88.8 9.9 %collective-permute-start.8 = (bf16[128,1024]{1,0:T(8,128)(2,1)S(1)}, bf16[128,1024]{1,0:T(8,128)(2,1)S(1)}, u32[]{:S(2)}, u32[]{:S(2)}) collective-permute-start(bf16[128,1024]{1,0:T(8,128)(2,1)S(1)} %get-tuple-element.34), channel_id=1, source_target_pairs={{0,24},{8,0},{16,8},{24,16},{1,25},{9,1},{17,9},{25,17},{2,26},{10... | collective-permute-start | bytes 786440 | tf_op jit(solution)/shard_map/ppermute | solution.py:39
  89.6 24.0 %collective-permute-start.7 = (bf16[128,1024]{1,0:T(8,128)(2,1)S(1)}, bf16[128,1024]{1,0:T(8,128)(2,1)S(1)}, u32[]{:S(2)}, u32[]{:S(2)}) collective-permute-start(bf16[128,1024]{1,0:T(8,128)(2,1)S(1)} %get-tuple-element.35), channel_id=1, source_target_pairs={{0,16},{8,24},{16,0},{24,8},{1,17},{9,25},{17,1},{25,9},{2,18},{10... | collective-permute-start | bytes 786440 | tf_op jit(solution)/shard_map/ppermute | solution.py:39
  89.9 23.6 %collective-permute-start.6 = (bf16[128,1024]{1,0:T(8,128)(2,1)S(1)}, bf16[128,1024]{1,0:T(8,128)(2,1)S(1)}, u32[]{:S(2)}, u32[]{:S(2)}) collective-permute-start(bf16[128,1024]{1,0:T(8,128)(2,1)S(1)} %get-tuple-element.36), channel_id=1, source_target_pairs={{0,8},{8,16},{16,24},{24,0},{1,9},{9,17},{17,25},{25,1},{2,10},{10... | collective-permute-start | bytes 786440 | tf_op jit(solution)/shard_map/ppermute | solution.py:39
  114.7 4.5 %copy-start.5 = (f32[128,1024]{1,0:T(8,128)S(1)}, f32[128,1024]{1,0:T(8,128)}, u32[]{:S(2)}) copy-start(f32[128,1024]{1,0:T(8,128)} %copy-done.4) | copy-start | bytes 1572868
  132.3 53.9 %all-to-all-start.2 = ((bf16[8,128,1024]{2,1,0:T(8,128)(2,1)}), bf16[8,128,1024]{2,1,0:T(8,128)(2,1)}, u32[]{:S(2)}, u32[]{:S(2)}) async-start(bf16[8,128,1024]{2,1,0:T(8,128)(2,1)} %broadcast_in_dim.134), calls=%async_computation.2 | async-start | bytes 4194304 | tf_op jit(solution)/shard_map/all_to_all | solution.py:137
  136.8 114.1 %reduce-scatter.2.cloned.1.call-start = ((), (), s32[]{:S(2)}) async-start(), calls=%async_computation.5 | async-start | bytes 1310720 | tf_op jit(solution)/shard_map/reduce_scatter | solution.py:150
  216.1 3.5 %copy-start = (f32[1024,1024]{1,0:T(8,128)S(1)}, f32[1024,1024]{1,0:T(8,128)}, u32[]{:S(2)}) copy-start(f32[1024,1024]{1,0:T(8,128)} %all-gather.4.cloned.1.call-done) | copy-start | bytes 12582916
  219.5 1.6 copy-start.9
  220.4 3.0 %copy-start.1 = (bf16[1024,1024]{1,0:T(8,128)(2,1)}, bf16[1024,1024]{1,0:T(8,128)(2,1)S(1)}, u32[]{:S(2)}) copy-start(bf16[1024,1024]{1,0:T(8,128)(2,1)S(1)} %fusion.2) | copy-start | bytes 6291460
  (3 other events, 2.7 us)
Sparse Core Ops, SparseCore 0:
  13.2 39.3 all-gather.3
  75.3 131.2 all-gather.5
  223.5 27.2 reduce-scatter.1
